TPU v7x, 128 devices: a whole 4x4x4 slice. The times are simulated.
128 devices in a mesh: tok: 16 (over y, x), head: 8 (over z, core).
Axes of the slice: x: 4, y: 4, z: 4, core: 2. Of those that a mesh axis runs over, the one named last changes fastest.
Arguments:
- tokens: bfloat16 [8192, 8192], P('tok', 'head'), may hold values from -60 to 60
- gain: bfloat16 [8192], P('head'), may hold values from 0.5 to 2
- w_query: bfloat16 [8192, 8, 512], P(('head', 'tok')), may hold values from -0.125 to 0.125
- w_key: bfloat16 [8192, 8, 128], P(('head', 'tok')), may hold values from -0.0625 to 0.0625
- w_value: bfloat16 [8192, 8, 128], P(('head', 'tok')), may hold values from -0.5 to 0.5
- group_ids: int32 [8192, 1], P('tok'), may hold values from 0 to 15; in each aligned block of 512 rows (0 to 511, 512 to 1023, ...) at most 64 rows name the same one
- key_pages: bfloat16 [1024, 128, 8, 128], P('tok', None, 'head'), may hold values from -42 to 42
- value_pages: bfloat16 [1024, 128, 8, 128], P('tok', None, 'head'), may hold values from -48 to 48
- page_table: int32 [16, 32], P('tok'), may hold values from 0 to 1023, as said below
Outputs:
- attention: bfloat16 [8192, 4096], P('tok', 'head')
Inputs may be any that keep to these rules, and one draw needn't show every extreme that they name: `group_ids`: among the 512 tokens of one index of tok (aligned blocks of rows), no group appears more than 64 times, a bound that some block reaches. `page_table`: row g lists 32 different pages, all in g * 64 to (g + 1) * 64 - 1, among them the first and the last page of that range.
All inputs are finite; a program needn't handle non-finite values.
Results may differ from a plain program's by a relative error of at most 0.0085.
The roundings to bfloat16 on the way count: a program that leaves them out, or rounds other values in their place, can miss the bound.
Values may be sent and summed in bfloat16 or wider, within the bound.
No kernel may reach another device: no remote copies, remote signals or barrier semaphores. Data moves between devices by JAX's collectives and lax.ppermute only.
A program may use at most 128 MiB of HBM per device.

v0:
```python
import math
import jax
import jax.numpy as jnp
from jax import lax
from jax.sharding import PartitionSpec as P

EPS = 1e-05
THETA = 10000.0


def rotate(values, positions):
    halfway = values.shape[-1] // 2
    frequency = jnp.exp(
        -math.log(THETA) * 2.0 * jnp.arange(halfway, dtype=jnp.float32) / values.shape[-1]
    )
    angles = positions.astype(jnp.float32)[:, None] * frequency[None, :]
    cosine = jnp.cos(angles)[:, None, :]
    sine_part = jnp.sin(angles)[:, None, :]
    leading = values[..., :halfway].astype(jnp.float32)
    trailing = values[..., halfway:].astype(jnp.float32)
    return jnp.concatenate(
        [leading * cosine - trailing * sine_part, trailing * cosine + leading * sine_part], axis=-1
    ).astype(jnp.bfloat16)


def attend(
    queries, query_rank, prefix_keys, prefix_values, new_keys, new_values, key_rank, key_live
):
    scaling = 1.0 / math.sqrt(queries.shape[-1])
    before = (
        jnp.einsum("bhd,pd->bhp", queries, prefix_keys, preferred_element_type=jnp.float32)
        * scaling
    )
    inside = (
        jnp.einsum("bhd,sd->bhs", queries, new_keys, preferred_element_type=jnp.float32) * scaling
    )
    allowed = key_live[None, :] & (key_rank[None, :] <= query_rank[:, None])
    inside = jnp.where(allowed[:, None, :], inside, -jnp.inf)
    highest = jnp.maximum(jnp.max(before, axis=-1), jnp.max(inside, axis=-1))
    expo_before = jnp.exp(before - highest[..., None])
    expo_inside = jnp.exp(inside - highest[..., None])
    totals = jnp.sum(expo_before, axis=-1) + jnp.sum(expo_inside, axis=-1)
    mixed = jnp.einsum(
        "bhp,pd->bhd",
        expo_before.astype(jnp.bfloat16),
        prefix_values,
        preferred_element_type=jnp.float32,
    )
    mixed = mixed + jnp.einsum(
        "bhs,sd->bhd",
        expo_inside.astype(jnp.bfloat16),
        new_values,
        preferred_element_type=jnp.float32,
    )
    return (mixed / totals[..., None]).astype(jnp.bfloat16)


def row_norm(tokens, gain, full_width):
    values_wide = tokens.astype(jnp.float32)
    squares = lax.psum(jnp.sum(values_wide * values_wide, axis=1), "head")
    factor = lax.rsqrt(squares / full_width + EPS)
    return (values_wide * factor[:, None] * gain.astype(jnp.float32)[None, :]).astype(jnp.bfloat16)


def body(tokens, gain, w_query, w_key, w_value, group_ids, key_pages, value_pages, page_table):
    row_count = tokens.shape[0]
    n_tok = lax.axis_size("tok")
    n_head = lax.axis_size("head")
    head_size = key_pages.shape[-1]
    query_width = w_query.shape[2]
    group_heads = query_width // head_size
    full_width = tokens.shape[1] * n_head
    capacity = 2 * row_count // n_tok
    normed = row_norm(tokens, gain, full_width)
    weights_local = jnp.concatenate([w_query, w_key, w_value], axis=2)
    gathered = lax.all_gather(weights_local, "tok", axis=0, tiled=True)
    group_count = row_count * lax.axis_size("head") // row_count
    joined = jnp.einsum("rd,dnc->nrc", normed, gathered, preferred_element_type=jnp.float32)
    projected = lax.psum_scatter(
        joined.reshape(group_count * row_count, joined.shape[2]),
        "head",
        scatter_dimension=0,
        tiled=True,
    )
    projected_low = projected.astype(jnp.bfloat16)
    width_all = projected_low.shape[1]
    group_of = group_ids[:, 0]
    member = (group_of[:, None] == jnp.arange(n_tok, dtype=jnp.int32)[None, :]).astype(jnp.int32)
    local_rank = jnp.sum((jnp.cumsum(member, axis=0) - member) * member, axis=1)
    slot_index = group_of * capacity + local_rank
    counts_local = jnp.sum(member, axis=0).astype(jnp.bfloat16)
    outgoing = (
        jnp.zeros((n_tok * capacity, width_all), jnp.bfloat16).at[slot_index].set(projected_low)
    )
    count_rows = jnp.broadcast_to(counts_local[:, None, None], (n_tok, 16, width_all))
    outgoing = jnp.concatenate([outgoing.reshape(n_tok, capacity, width_all), count_rows], axis=1)
    arrived_all = lax.all_to_all(outgoing, "tok", split_axis=0, concat_axis=0, tiled=True)
    block_counts = arrived_all[:, capacity, 0].astype(jnp.int32)
    arrived = arrived_all[:, :capacity, :]
    slot_total = n_tok * capacity
    arrived = arrived.reshape(slot_total, width_all)
    live_count = (
        (jnp.arange(capacity, dtype=jnp.int32)[None, :] < block_counts[:, None])
        .astype(jnp.int32)
        .reshape(slot_total)
    )
    key_live = live_count > 0
    slot_rank = jnp.cumsum(live_count) - live_count
    prefix_length = page_table.shape[1] * key_pages.shape[1]
    positions = prefix_length + slot_rank
    rotated_queries = rotate(
        arrived[:, :query_width].reshape(slot_total, group_heads, head_size), positions
    )
    rotated_keys = rotate(
        arrived[:, query_width : query_width + head_size].reshape(slot_total, 1, head_size),
        positions,
    )[:, 0, :]
    slot_values = arrived[:, query_width + head_size :]
    local_pages = page_table[0] - lax.axis_index("tok") * key_pages.shape[0]
    prefix_keys = jnp.take(key_pages[:, :, 0, :], local_pages, axis=0).reshape(
        prefix_length, head_size
    )
    prefix_values = jnp.take(value_pages[:, :, 0, :], local_pages, axis=0).reshape(
        prefix_length, head_size
    )
    block_size = min(128, slot_total)

    def one_block(blocked):
        return attend(
            blocked[0],
            blocked[1],
            prefix_keys,
            prefix_values,
            rotated_keys,
            slot_values,
            slot_rank,
            key_live,
        )

    attended = lax.map(
        one_block,
        (
            rotated_queries.reshape(slot_total // block_size, block_size, group_heads, head_size),
            slot_rank.reshape(slot_total // block_size, block_size),
        ),
    )
    returned = lax.all_to_all(
        attended.reshape(n_tok, capacity, query_width),
        "tok",
        split_axis=0,
        concat_axis=0,
        tiled=True,
    )
    return returned.reshape(n_tok * capacity, query_width)[slot_index]


def solution(mesh):
    placed = (
        P("tok", "head"),
        P("head"),
        P(("head", "tok"), None, None),
        P(("head", "tok"), None, None),
        P(("head", "tok"), None, None),
        P("tok", None),
        P("tok", None, "head", None),
        P("tok", None, "head", None),
        P("tok", None),
    )
    return jax.shard_map(
        body, mesh=mesh, in_specs=placed, out_specs=P("tok", "head"), check_vma=False
    )
```

profile of v0, /device:TPU:32, one launch (start us, length us, event | category | flops | bytes accessed | tf_op | source)
XLA Modules:
  0.0 343.7 jit_solution(11092186876331091009)
XLA Ops:
  11.1 12.5 %psum.7 = f32[512]{0:T(512)S(1)} all-reduce(f32[512]{0:T(512)S(1)} %fusion.33), channel_id=1, replica_groups=mesh['tok'=16,'head'=8] {'head'}, use_global_device_ids=true, to_apply=%region_4.5 | all-reduce | flops 512 | bytes 4096 | tf_op jit(solution)/shard_map/psum | solution.py:60
  23.6 78.9 %all-gather.2.cloned.1.call-done = bf16[1024,8,768]{2,0,1:T(8,128)(2,1)} async-done(((bf16[64,8,768]{2,0,1:T(8,128)(2,1)}), bf16[1024,8,768]{2,0,1:T(8,128)(2,1)}) %all-gather.2.cloned.1.call-update) | async-done | bytes 12582928 | tf_op jit(solution)/shard_map/all_gather | solution.py:76
  102.5 14.4 %fusion.41 = f32[8,768,512]{1,2,0:T(8,128)} fusion(bf16[1024,8,768]{2,0,1:T(8,128)(2,1)} %all-gather.2.cloned.1.call-done, bf16[512,1024]{1,0:T(8,128)(2,1)S(1)} %copy-done.3, f32[1024]{0:T(1024)S(1)} %convert_element_type.95, f32[512]{0:T(512)S(1)} %add_rsqrt_fusion), kind=kOutput, calls=%fused_computation.59 | convolution fusion | flops 6444548096 | bytes 26220544 | tf_op jit(solution)/shard_map/rd,dnc->nrc/dot_general | solution.py:78
  119.2 67.6 %reduce-scatter.2.cloned.1.call-done = f32[512,768]{1,0:T(8,128)} async-done(((f32[4096,768]{1,0:T(8,128)}), f32[512,768]{1,0:T(8,128)}) %reduce-scatter.2.cloned.1.call-update) | async-done | bytes 1572880 | tf_op jit(solution)/shard_map/reduce_scatter | solution.py:79
  186.7 4.6 %scatter_custom_fusion = bf16[1024,768]{1,0:T(8,128)(2,1)} fusion(s32[512]{0:T(512)S(1)} %bitcast.115, f32[512,768]{1,0:T(8,128)} %reduce-scatter.2.cloned.1.call-done, bf16[]{:T(256)} %constant.32.clone.1), kind=kCustom, calls=%fused_computation.66 | custom fusion | flops 393216 | bytes 3145730 | tf_op jit(solution)/shard_map/scatter | solution.py:93
  191.5 2.8 pad_maximum_fusion
  194.3 7.2 %all-to-all-start = ((bf16[16,80,768]{2,1,0:T(8,128)(2,1)}), bf16[16,80,768]{2,1,0:T(8,128)(2,1)}, u32[]{:S(2)}, u32[]{:S(2)}) async-start(bf16[16,80,768]{2,1,0:T(8,128)(2,1)} %pad_maximum_fusion), calls=%async_computation.1 | async-start | bytes 3932160 | tf_op jit(solution)/shard_map/all_to_all | solution.py:97
  202.4 3.3 gather_fusion.2
  207.2 27.9 %all-to-all-done = bf16[16,80,768]{2,1,0:T(8,128)(2,1)} async-done(((bf16[16,80,768]{2,1,0:T(8,128)(2,1)}), bf16[16,80,768]{2,1,0:T(8,128)(2,1)}, u32[]{:S(2)}, u32[]{:S(2)}) %all-to-all-start) | async-done | bytes 1966112 | tf_op jit(solution)/shard_map/all_to_all | solution.py:97
  236.4 1.6 slice.60
  239.6 1.8 multiply_cosine_fusion.1
  241.4 3.1 fusion.57
  245.9 1.6 fusion.37
  248.8 1.7 copy.28
  251.7 58.3 %while.11 = (s32[]{:T(128)}, bf16[8,128,4,128]{3,2,1,0:T(4,128)(2,1)}, bf16[8,128,4,128]{3,1,2,0:T(8,128)(2,1)S(1)}, bf16[4096,128]{1,0:T(8,128)(2,1)S(1)}, s32[...) while((s32[]{:T(128)}, ...), condition=%wide.region_15.17_spmd.clone, body=%wide.region_10.16_spmd.clone.sunk | while | flops 1365182464 | bytes 36886740 | solution.py:140
  254.6 1.5 fusion.84
  256.1 1.5 fusion.83
  261.9 1.5 fusion.84
  263.4 1.5 fusion.83
  269.2 1.5 fusion.84
  270.7 1.5 fusion.83
  276.4 1.5 fusion.84
  283.7 1.5 fusion.84
  285.2 1.5 fusion.83
  291.0 1.5 fusion.84
  298.3 1.5 fusion.84
  299.8 1.5 fusion.83
  305.6 1.5 fusion.84
  310.0 2.3 reshape.292
  312.3 3.7 %all-to-all-start.1 = ((bf16[16,64,512]{2,1,0:T(8,128)(2,1)}), bf16[16,64,512]{2,1,0:T(8,128)(2,1)S(1)}, u32[]{:S(2)}, u32[]{:S(2)}) async-start(bf16[16,64,512]{2,1,0:T(8,128)(2,1)} %reshape.292), calls=%async_computation.2 | async-start | bytes 2097152 | tf_op jit(solution)/shard_map/all_to_all | solution.py:147
  316.0 18.2 %all-to-all-done.1 = bf16[16,64,512]{2,1,0:T(8,128)(2,1)S(1)} async-done(((bf16[16,64,512]{2,1,0:T(8,128)(2,1)}), bf16[16,64,512]{2,1,0:T(8,128)(2,1)S(1)}, u32[]{:S(2)}, u32[]{:S(2)}) %all-to-all-start.1) | async-done | bytes 1048608 | tf_op jit(solution)/shard_map/all_to_all | solution.py:147
  334.2 2.6 gather_fusion
  (178 shorter events, 54.5 us)
Async XLA Ops:
  6.5 195.1 %copy-start = (bf16[64,128,1,128]{3,1,2,0:T(8,128)(2,1)S(1)}, bf16[64,128,1,128]{3,1,2,0:T(8,128)(2,1)}, u32[]{:S(2)}) copy-start(bf16[64,128,1,128]{3,1,2,0:T(8,128)(2,1)} %param.19) | copy-start | bytes 6291460
  6.5 4.2 %copy-start.6 = (bf16[1024]{0:T(1024)(128)(2,1)S(1)}, bf16[1024]{0:T(1024)(128)(2,1)}, u32[]{:S(2)}) copy-start(bf16[1024]{0:T(1024)(128)(2,1)} %param.14) | copy-start | bytes 6148
  6.5 4.3 %copy-start.3 = (bf16[512,1024]{1,0:T(8,128)(2,1)S(1)}, bf16[512,1024]{1,0:T(8,128)(2,1)}, u32[]{:S(2)}) copy-start(bf16[512,1024]{1,0:T(8,128)(2,1)} %param.13) | copy-start | bytes 3145732
  6.5 96.0 %all-gather.2.cloned.1.call-start = ((), (), s32[]{:S(2)}) async-start(), calls=%async_computation.3 | async-start | bytes 13369344 | tf_op jit(solution)/shard_map/all_gather | solution.py:76
  10.7 176.0 %reduce-scatter.2.cloned.1.call-start = ((), (), s32[]{:S(2)}) async-start(), calls=%async_computation.4 | async-start | bytes 14155776 | tf_op jit(solution)/shard_map/reduce_scatter | solution.py:79
  116.9 0.7 copy-start.5
  194.3 7.3 %copy-start.7 = (s32[1,32]{1,0:T(1,128)S(1)}, s32[1,32]{1,0:T(1,128)}, u32[]{:S(2)}) copy-start(s32[1,32]{1,0:T(1,128)} %param.21) | copy-start | bytes 388
  194.3 40.8 %all-to-all-start = ((bf16[16,80,768]{2,1,0:T(8,128)(2,1)}), bf16[16,80,768]{2,1,0:T(8,128)(2,1)}, u32[]{:S(2)}, u32[]{:S(2)}) async-start(bf16[16,80,768]{2,1,0:T(8,128)(2,1)} %pad_maximum_fusion), calls=%async_computation.1 | async-start | bytes 3932160 | tf_op jit(solution)/shard_map/all_to_all | solution.py:97
  244.6 1.3 copy-start.2
  256.1 1.5 copy-start.4
  263.4 1.5 copy-start.4
  270.7 1.5 copy-start.4
  277.9 1.5 copy-start.4
  285.2 1.5 copy-start.4
  292.5 1.5 copy-start.4
  299.8 1.5 copy-start.4
  307.1 1.5 copy-start.4
  312.3 21.9 %all-to-all-start.1 = ((bf16[16,64,512]{2,1,0:T(8,128)(2,1)}), bf16[16,64,512]{2,1,0:T(8,128)(2,1)S(1)}, u32[]{:S(2)}, u32[]{:S(2)}) async-start(bf16[16,64,512]{2,1,0:T(8,128)(2,1)} %reshape.292), calls=%async_computation.2 | async-start | bytes 2097152 | tf_op jit(solution)/shard_map/all_to_all | solution.py:147
  334.2 2.6 copy-start.1
Sparse Core Ops, SparseCore 0:
  10.9 91.6 all-gather.1
  117.1 69.6 reduce-scatter.1
where the time goes:
time: 344 us
  waiting for transfers between devices  193 us (56%)
  matrix products  46.8 us (14%)
  other arithmetic  40.8 us (12%)
  local copies, waits for them, and re-layouts  26 us (8%)
  between operations  13.6 us (4%)
  blocking collectives  12.5 us (4%)
  starting transfers between devices  10.9 us (3%)
    all_gather x1, waiting for transfers between devices, body(): gathered = lax.all_gather(weights_local, 'tok', axis=0, tiled=True)  78.9 us
    reduce_scatter x1, waiting for transfers between devices, body(): lax.psum_scatter(joined.reshape(group_count * row_count, joined.shape[2])...  67.6 us
    all_to_all x1, waiting for transfers between devices, body(): lax.all_to_all(outgoing, 'tok', split_axis=0, concat_axis=0, tiled=True)  27.9 us
    all_to_all x1, waiting for transfers between devices, body(): lax.all_to_all(attended.reshape(n_tok, capacity, query_width), 'tok', spl...  18.2 us
    reduce_sum x16, other arithmetic, attend(): totals = jnp.sum(expo_before, axis=-1) + jnp.sum(expo_inside, axis=-1)  16.8 us
    dot_general x1, matrix products, body(): jnp.einsum('rd,dnc->nrc', normed, gathered, preferred_element_type=jnp.fl...  14.4 us
    psum x1, blocking collectives, row_norm(): squares = lax.psum(jnp.sum(values_wide * values_wide, axis=1), 'head')  12.5 us
    dot_general x8, matrix products, attend(): jnp.einsum('bhp,pd->bhd', expo_before.astype(jnp.bfloat16), prefix_values...  11.8 us
  transfers between devices with their start and end apart: 4, of which 4 were waited for; matrix products, arithmetic and copies ran while one was open for 2% of the time, Pallas kernels for 0%

commit v1 on v0

--- a/solution.py
+++ b/solution.py
@@ -73,7 +73,9 @@
     capacity = 2 * row_count // n_tok
     normed = row_norm(tokens, gain, full_width)
     weights_local = jnp.concatenate([w_query, w_key, w_value], axis=2)
-    gathered = lax.all_gather(weights_local, "tok", axis=0, tiled=True)
+    gathered = jnp.concatenate(
+        lax.all_to_all(jnp.stack([weights_local] * lax.axis_size("tok")), "tok", 0, 0), axis=0
+    )
     group_count = row_count * lax.axis_size("head") // row_count
     joined = jnp.einsum("rd,dnc->nrc", normed, gathered, preferred_element_type=jnp.float32)
     projected = lax.psum_scatter(

time: 344 us -> 451 us (1.31)
  waiting for transfers between devices: 193 us -> 287 us
  local copies, waits for them, and re-layouts: 26 us -> 35.5 us
  starting transfers between devices: 10.9 us -> 18.1 us
  matrix products: 46.8 us -> 41.8 us
    all_to_all x0 -> x1, waiting for transfers between devices: none -> 174 us  [body(): lax.all_to_all(jnp.stack([weights_local] * lax.axis_size('tok')), 'tok',...]
    all_gather x1 -> x0, waiting for transfers between devices: 78.9 us -> none  [body(): gathered = lax.all_gather(weights_local, 'tok', axis=0, tiled=True)]
    all_to_all x0 -> x1, starting transfers between devices: none -> 7.21 us  [body(): lax.all_to_all(jnp.stack([weights_local] * lax.axis_size('tok')), 'tok',...]
    all_to_all x0 -> x1, local copies, waits for them, and re-layouts: none -> 6.52 us  [body(): lax.all_to_all(jnp.stack([weights_local] * lax.axis_size('tok')), 'tok',...]
    another operation x3 -> x4, local copies, waits for them, and re-layouts: 0.2 us -> 6.24 us  [the longest x1 6.05 us: body(): jnp.stack([weights_local] * lax.axis_size('tok'))]
    dot_general x1, matrix products: 14.4 us -> 9.34 us  [body(): jnp.einsum('rd,dnc->nrc', normed, gathered, preferred_element_type=jnp.fl...]
where the time goes in v1:
time: 451 us
  waiting for transfers between devices  287 us (64%)
  matrix products  41.8 us (9%)
  other arithmetic  41.2 us (9%)
  local copies, waits for them, and re-layouts  35.5 us (8%)
  starting transfers between devices  18.1 us (4%)
  between operations  13.6 us (3%)
  blocking collectives  12.6 us (3%)
    all_to_all x1, waiting for transfers between devices, body(): lax.all_to_all(jnp.stack([weights_local] * lax.axis_size('tok')), 'tok',...  174 us
    reduce_scatter x1, waiting for transfers between devices, body(): lax.psum_scatter(joined.reshape(group_count * row_count, joined.shape[2])...  67.3 us
    all_to_all x1, waiting for transfers between devices, body(): lax.all_to_all(outgoing, 'tok', split_axis=0, concat_axis=0, tiled=True)  27.9 us
    all_to_all x1, waiting for transfers between devices, body(): lax.all_to_all(attended.reshape(n_tok, capacity, query_width), 'tok', spl...  18.2 us
    reduce_sum x16, other arithmetic, attend(): totals = jnp.sum(expo_before, axis=-1) + jnp.sum(expo_inside, axis=-1)  16.8 us
    psum x1, blocking collectives, row_norm(): squares = lax.psum(jnp.sum(values_wide * values_wide, axis=1), 'head')  12.6 us
    dot_general x8, matrix products, attend(): jnp.einsum('bhp,pd->bhd', expo_before.astype(jnp.bfloat16), prefix_values...  11.8 us
    dot_general x8, matrix products, attend(): jnp.einsum('bhd,pd->bhp', queries, prefix_keys, preferred_element_type=jn...  10.7 us
  transfers between devices with their start and end apart: 4, of which 4 were waited for; matrix products, arithmetic and copies ran while one was open for 2% of the time, Pallas kernels for 0%

profile of v1, /device:TPU:32, one launch (start us, length us, event | category | flops | bytes accessed | tf_op | source)
XLA Modules:
  0.0 450.8 jit_solution(7649650904428789595)
XLA Ops:
  8.1 6.0 %stack.2 = bf16[16,64,8,768]{3,1,2,0:T(8,128)(2,1)} broadcast(bf16[64,8,768]{2,0,1:T(8,128)(2,1)S(1)} %copy.25), dimensions={1,2,3} | broadcast | bytes 13369344 | tf_op jit(solution)/shard_map/stack | solution.py:77
  14.1 7.2 %all-to-all-start = ((bf16[16,64,8,768]{3,1,2,0:T(8,128)(2,1)}), bf16[16,64,8,768]{3,1,2,0:T(8,128)(2,1)}, u32[]{:S(2)}, u32[]{:S(2)}) async-start(bf16[16,64,8,768]{3,1,2,0:T(8,128)(2,1)} %stack.2), calls=%async_computation | async-start | bytes 25165824 | tf_op jit(solution)/shard_map/all_to_all | solution.py:77
  21.7 12.6 %psum.7 = f32[512]{0:T(512)S(1)} all-reduce(f32[512]{0:T(512)S(1)} %fusion.33), channel_id=1, replica_groups=mesh['tok'=16,'head'=8] {'head'}, use_global_device_ids=true, to_apply=%region_4.5 | all-reduce | flops 512 | bytes 4096 | tf_op jit(solution)/shard_map/psum | solution.py:60
  34.3 174.0 %all-to-all-done = bf16[16,64,8,768]{3,1,2,0:T(8,128)(2,1)} async-done(((bf16[16,64,8,768]{3,1,2,0:T(8,128)(2,1)}), bf16[16,64,8,768]{3,1,2,0:T(8,128)(2,1)}, u32[]{:S(2)}, u32[]{:S(2)}) %all-to-all-start) | async-done | bytes 12582944 | tf_op jit(solution)/shard_map/all_to_all | solution.py:77
  208.4 6.5 %copy.26 = bf16[16,64,8,768]{3,1,0,2:T(8,128)(2,1)S(1)} copy(bf16[16,64,8,768]{3,1,2,0:T(8,128)(2,1)} %all-to-all-done) | data formatting | bytes 25165824 | tf_op jit(solution)/shard_map/all_to_all | solution.py:77
  214.9 9.3 %fusion.41 = f32[8,768,512]{1,2,0:T(8,128)} fusion(bf16[1024,8,768]{2,0,1:T(8,128)(2,1)S(1)} %bitcast.105, bf16[512,1024]{1,0:T(8,128)(2,1)S(1)} %copy-done.3, f32[1024]{0:T(1024)S(1)} %convert_element_type.95, f32[512]{0:T(512)S(1)} %add_rsqrt_fusion), kind=kOutput, calls=%fused_computation.59 | convolution fusion | flops 6444548096 | bytes 26220544 | tf_op jit(solution)/shard_map/rd,dnc->nrc/dot_general | solution.py:80
  226.5 67.3 %reduce-scatter.2.cloned.1.call-done = f32[512,768]{1,0:T(8,128)} async-done(((f32[4096,768]{1,0:T(8,128)}), f32[512,768]{1,0:T(8,128)}) %reduce-scatter.2.cloned.1.call-update) | async-done | bytes 1572880 | tf_op jit(solution)/shard_map/reduce_scatter | solution.py:81
  293.8 4.6 %scatter_custom_fusion = bf16[1024,768]{1,0:T(8,128)(2,1)} fusion(s32[512]{0:T(512)S(1)} %bitcast.117, f32[512,768]{1,0:T(8,128)} %reduce-scatter.2.cloned.1.call-done, bf16[]{:T(256)} %constant.32.clone.1), kind=kCustom, calls=%fused_computation.66 | custom fusion | flops 393216 | bytes 3145730 | tf_op jit(solution)/shard_map/scatter | solution.py:95
  298.6 2.8 pad_maximum_fusion
  301.4 7.2 %all-to-all-start.1 = ((bf16[16,80,768]{2,1,0:T(8,128)(2,1)}), bf16[16,80,768]{2,1,0:T(8,128)(2,1)}, u32[]{:S(2)}, u32[]{:S(2)}) async-start(bf16[16,80,768]{2,1,0:T(8,128)(2,1)} %pad_maximum_fusion), calls=%async_computation.2 | async-start | bytes 3932160 | tf_op jit(solution)/shard_map/all_to_all | solution.py:99
  309.5 3.3 gather_fusion.2
  314.2 27.9 %all-to-all-done.1 = bf16[16,80,768]{2,1,0:T(8,128)(2,1)} async-done(((bf16[16,80,768]{2,1,0:T(8,128)(2,1)}), bf16[16,80,768]{2,1,0:T(8,128)(2,1)}, u32[]{:S(2)}, u32[]{:S(2)}) %all-to-all-start.1) | async-done | bytes 1966112 | tf_op jit(solution)/shard_map/all_to_all | solution.py:99
  343.4 1.6 slice.60
  346.7 1.8 multiply_cosine_fusion.1
  348.5 3.1 fusion.57
  353.0 1.6 fusion.37
  355.9 1.7 copy.29
  358.8 58.3 %while.11 = (s32[]{:T(128)}, bf16[8,128,4,128]{3,2,1,0:T(4,128)(2,1)}, bf16[8,128,4,128]{3,1,2,0:T(8,128)(2,1)S(1)}, bf16[4096,128]{1,0:T(8,128)(2,1)S(1)}, s32[...) while((s32[]{:T(128)}, ...), condition=%wide.region_15.17_spmd.clone, body=%wide.region_10.16_spmd.clone.sunk | while | flops 1365182464 | bytes 36886740 | solution.py:142
  361.6 1.5 fusion.84
  363.2 1.5 fusion.83
  368.9 1.5 fusion.84
  370.4 1.5 fusion.83
  376.2 1.5 fusion.84
  383.5 1.5 fusion.84
  390.8 1.5 fusion.84
  398.1 1.5 fusion.84
  405.4 1.5 fusion.84
  412.6 1.5 fusion.84
  417.1 2.3 reshape.298
  419.4 3.7 all-to-all-start.2
  423.0 18.2 %all-to-all-done.2 = bf16[16,64,512]{2,1,0:T(8,128)(2,1)S(1)} async-done(((bf16[16,64,512]{2,1,0:T(8,128)(2,1)}), bf16[16,64,512]{2,1,0:T(8,128)(2,1)S(1)}, u32[]{:S(2)}, u32[]{:S(2)}) %all-to-all-start.2) | async-done | bytes 1048608 | tf_op jit(solution)/shard_map/all_to_all | solution.py:149
  441.3 2.6 gather_fusion
  (177 shorter events, 56.3 us)
Async XLA Ops:
  6.5 302.2 %copy-start = (bf16[64,128,1,128]{3,1,2,0:T(8,128)(2,1)S(1)}, bf16[64,128,1,128]{3,1,2,0:T(8,128)(2,1)}, u32[]{:S(2)}) copy-start(bf16[64,128,1,128]{3,1,2,0:T(8,128)(2,1)} %param.19) | copy-start | bytes 6291460
  14.1 7.3 %copy-start.6 = (bf16[1024]{0:T(1024)(128)(2,1)S(1)}, bf16[1024]{0:T(1024)(128)(2,1)}, u32[]{:S(2)}) copy-start(bf16[1024]{0:T(1024)(128)(2,1)} %param.14) | copy-start | bytes 6148
  14.1 7.3 %copy-start.3 = (bf16[512,1024]{1,0:T(8,128)(2,1)S(1)}, bf16[512,1024]{1,0:T(8,128)(2,1)}, u32[]{:S(2)}) copy-start(bf16[512,1024]{1,0:T(8,128)(2,1)} %param.13) | copy-start | bytes 3145732
  14.1 194.2 %all-to-all-start = ((bf16[16,64,8,768]{3,1,2,0:T(8,128)(2,1)}), bf16[16,64,8,768]{3,1,2,0:T(8,128)(2,1)}, u32[]{:S(2)}, u32[]{:S(2)}) async-start(bf16[16,64,8,768]{3,1,2,0:T(8,128)(2,1)} %stack.2), calls=%async_computation | async-start | bytes 25165824 | tf_op jit(solution)/shard_map/all_to_all | solution.py:77
  21.3 272.5 %reduce-scatter.2.cloned.1.call-start = ((), (), s32[]{:S(2)}) async-start(), calls=%async_computation.4 | async-start | bytes 14155776 | tf_op jit(solution)/shard_map/reduce_scatter | solution.py:81
  224.2 0.7 copy-start.5
  301.4 7.3 %copy-start.7 = (s32[1,32]{1,0:T(1,128)S(1)}, s32[1,32]{1,0:T(1,128)}, u32[]{:S(2)}) copy-start(s32[1,32]{1,0:T(1,128)} %param.21) | copy-start | bytes 388
  301.4 40.7 %all-to-all-start.1 = ((bf16[16,80,768]{2,1,0:T(8,128)(2,1)}), bf16[16,80,768]{2,1,0:T(8,128)(2,1)}, u32[]{:S(2)}, u32[]{:S(2)}) async-start(bf16[16,80,768]{2,1,0:T(8,128)(2,1)} %pad_maximum_fusion), calls=%async_computation.2 | async-start | bytes 3932160 | tf_op jit(solution)/shard_map/all_to_all | solution.py:99
  351.6 1.3 copy-start.2
  363.2 1.5 copy-start.4
  370.4 1.5 copy-start.4
  377.7 1.5 copy-start.4
  385.0 1.5 copy-start.4
  392.3 1.5 copy-start.4
  399.6 1.5 copy-start.4
  406.9 1.5 copy-start.4
  414.2 1.5 copy-start.4
  419.4 21.9 %all-to-all-start.2 = ((bf16[16,64,512]{2,1,0:T(8,128)(2,1)}), bf16[16,64,512]{2,1,0:T(8,128)(2,1)S(1)}, u32[]{:S(2)}, u32[]{:S(2)}) async-start(bf16[16,64,512]{2,1,0:T(8,128)(2,1)} %reshape.298), calls=%async_computation.3 | async-start | bytes 2097152 | tf_op jit(solution)/shard_map/all_to_all | solution.py:149
  441.3 2.6 copy-start.1
Sparse Core Ops, SparseCore 0:
  224.4 69.3 reduce-scatter.1
